TPU v7x, 256 devices: a whole 4x4x8 slice. The times are simulated.
256 devices in a mesh: aa: 32 (over z, x), ba: 8 (over y, core).
Axes of the slice: x: 4, y: 4, z: 8, core: 2. Of those that a mesh axis runs over, the one named last changes fastest.
Arguments:
- snapshots: float32 [8192, 65536], P(('aa', 'ba')), may hold values from -125 to 125
Outputs:
- factors: float32 [8, 64, 64], replicated
- pod_modes: float32 [8, 64, 65536], P(None, None, ('aa', 'ba'))
All inputs are finite; a program needn't handle non-finite values.
Results may differ from a plain program's by a relative error of at most 0.000098.
Values sent between devices are 32-bit elements; how exact they have to be, the bound alone decides.
No kernel may reach another device: no remote copies, remote signals or barrier semaphores. Data moves between devices by JAX's collectives and lax.ppermute only.
A program may use at most 128 MiB of HBM per device.

v0:
```python
import math
import jax
import jax.numpy as jnp
from jax import lax
from jax.sharding import PartitionSpec as P

FREQS = 8


def spectral_rows(block_len, points, first, count):
    sample = first + jnp.arange(count, dtype=jnp.int32)
    harmonic = jnp.arange(1, FREQS + 1, dtype=jnp.int32)
    phase_turns = (sample[:, None] * harmonic[None, :] % block_len).astype(jnp.float32) * (
        2.0 * math.pi / block_len
    )
    full = jnp.arange(block_len, dtype=jnp.int32).astype(jnp.float32) * (2.0 * math.pi / block_len)
    full_window = 0.5 - 0.5 * jnp.cos(full)
    norm_scale = 1.0 / jnp.sqrt(points * jnp.sum(full_window * full_window))
    sample_angle = sample.astype(jnp.float32) * (2.0 * math.pi / block_len)
    window = 0.5 - 0.5 * jnp.cos(sample_angle)
    cosine = window[:, None] * jnp.cos(phase_turns) * norm_scale
    sine = -window[:, None] * jnp.sin(phase_turns) * norm_scale
    return jnp.stack([cosine, sine], axis=1)


def local(snapshots):
    time_dev, points = snapshots.shape
    n_aa = lax.axis_size("aa")
    n_ba = lax.axis_size("ba")
    pts_dev = points // (n_aa * n_ba)
    block_len = time_dev * n_ba
    u = lax.axis_index("ba")
    table = spectral_rows(block_len, points, u * time_dev, time_dev)
    arranged = snapshots.reshape(time_dev, n_aa, n_ba, pts_dev)
    partial = jnp.einsum("savq,sgf->vgfaq", arranged, table, precision=lax.Precision.HIGHEST)
    block_spec = lax.psum_scatter(partial, "ba", scatter_dimension=0, tiled=True)
    spectra = lax.all_to_all(block_spec, "aa", split_axis=3, concat_axis=0, tiled=True)
    blocks = spectra.shape[0]
    columns = 2 * blocks
    cols = jnp.transpose(spectra.reshape(blocks, 2, FREQS, pts_dev), (2, 0, 1, 3)).reshape(
        FREQS, columns, pts_dev
    )
    product = jnp.einsum("fip,fjp->fij", cols, cols, precision=lax.Precision.HIGHEST)
    gram_sum = lax.psum(product, ("aa", "ba"))
    lower_factor = jnp.linalg.cholesky(gram_sum)
    identity = jnp.broadcast_to(jnp.eye(columns, dtype=gram_sum.dtype), lower_factor.shape)
    inverse = lax.linalg.triangular_solve(lower_factor, identity, left_side=True, lower=True)
    pod_modes = math.sqrt(points) * jnp.einsum(
        "fij,fjp->fip", inverse, cols, precision=lax.Precision.HIGHEST
    )
    return (jnp.swapaxes(lower_factor, 1, 2), pod_modes)


def solution(mesh):
    placed = (P(("aa", "ba"), None),)
    return jax.shard_map(
        local,
        mesh=mesh,
        in_specs=placed,
        out_specs=(P(), P(None, None, ("aa", "ba"))),
        check_vma=False,
    )
```

profile of v0, /device:TPU:2, one launch (start us, length us, event | category | flops | bytes accessed | tf_op | source)
XLA Modules:
  0.0 479.1 jit_solution(12910174082356562652)
XLA Ops:
  7.2 0.0 all-reduce.6.cloned.1.call-start
  7.3 0.6 multiply_reduce_fusion
  8.6 5.9 %copy.38 = f32[4,8,256,256]{3,2,1,0:T(8,128)S(1)} copy(f32[4,8,256,256]{3,1,2,0:T(8,128)} %bitcast.42) | data formatting | bytes 16777216
  14.6 0.1 multiply_multiply_fusion.1
  14.7 0.0 copy-start
  14.7 9.2 %fusion.3 = f32[8,2,8,32,256]{4,2,0,3,1:T(8,128)} fusion(f32[32,32,8,256]{3,2,1,0:T(8,128)S(1)} %bitcast.41, f32[32,1,8]{0,2,1:T(8,128)S(1)} %get-tuple-element.13, f32[32,1,8]{0,2,1:T(8,128)S(1)} %get-tuple-element.12), kind=kOutput, calls=%fused_computation.3 | convolution fusion | flops 402653696 | bytes 12584960 | tf_op jit(solution)/shard_map/savq,sgf->vgfaq/dot_general | solution.py:35
  23.9 0.0 all-reduce.6.cloned.1.call-update
  23.9 0.0 copy-done
  23.9 0.6 dynamic-slice
  24.5 80.1 %all-reduce.6.cloned.1.call-done = f32[8,2,8,32,256]{4,2,0,3,1:T(8,128)} async-done(((f32[8,2,8,32,256]{4,2,0,3,1:T(8,128)}), f32[8,2,8,32,256]{4,2,0,3,1:T(8,128)}) %all-reduce.6.cloned.1.call-update) | async-done | bytes 4194320
  104.6 1.7 constant_dynamic-slice_fusion
  106.3 0.9 copy.25
  107.2 10.1 %all-to-all-start = ((f32[1,2,8,32,256]{4,2,0,1,3:T(8,128)}), f32[1,2,8,32,256]{4,2,0,1,3:T(8,128)S(1)}, u32[]{:S(2)}, u32[]{:S(2)}) async-start(f32[1,2,8,32,256]{4,2,0,1,3:T(8,128)} %copy.25), calls=%async_computation | async-start | bytes 1048576 | tf_op jit(solution)/shard_map/all_to_all | solution.py:37
  117.3 0.2 all-reduce.4.cloned.1.call-start
  117.6 14.8 %all-to-all-done = f32[1,2,8,32,256]{4,2,0,1,3:T(8,128)S(1)} async-done(((f32[1,2,8,32,256]{4,2,0,1,3:T(8,128)}), f32[1,2,8,32,256]{4,2,0,1,3:T(8,128)S(1)}, u32[]{:S(2)}, u32[]{:S(2)}) %all-to-all-start) | async-done | bytes 524320 | tf_op jit(solution)/shard_map/all_to_all | solution.py:37
  132.4 1.6 fusion.7
  134.0 0.0 all-reduce.4.cloned.1.call-update
  134.0 246.7 %all-reduce.4.cloned.1.call-done = f32[8,64,64]{1,2,0:T(8,128)} async-done(((f32[8,64,64]{1,2,0:T(8,128)}), f32[8,64,64]{1,2,0:T(8,128)}) %all-reduce.4.cloned.1.call-update) | async-done | bytes 131088 | tf_op jit(solution)/shard_map/psum | solution.py:44
  380.7 1.1 copy.29
  381.8 1.0 fusion.11
  382.8 46.9 %custom-call.7 = f32[8,64,64]{2,1,0:T(8,128)S(1)} custom-call(f32[8,64,64]{2,1,0:T(8,128)S(1)} %fusion.11), custom_call_target="Cholesky" | custom-call | tf_op jit(solution)/shard_map/jit(cholesky)/cholesky | solution.py:45
  429.8 0.1 compare_reduce_fusion
  429.9 0.1 select_bitcast_fusion
  430.0 39.3 %custom-call.8 = f32[8,1,64,64]{2,3,1,0:T(8,128)S(1)} custom-call(f32[8,1,64,64]{3,2,1,0:T(8,128)S(1)} %get-tuple-element.10), custom_call_target="InvertDiagBlocksLowerTriangular" | custom-call | tf_op jit(solution)/shard_map/triangular_solve | solution.py:47
  469.3 0.6 fusion.9
  469.9 1.5 convolution_multiply_fusion
  471.5 0.8 copy.32
  (7 shorter events, 0.1 us)
Async XLA Ops:
  7.2 97.5 %all-reduce.6.cloned.1.call-start = ((), (), s32[]{:S(2)}) async-start(), calls=%async_computation.2 | async-start | bytes 8388608
  14.7 9.2 %copy-start = (u32[256]{0:T(256)S(1)}, u32[256]{0:T(256)}, u32[]{:S(2)}) copy-start(u32[256]{0:T(256)} %constant.81) | copy-start | bytes 3076
  107.2 25.2 %all-to-all-start = ((f32[1,2,8,32,256]{4,2,0,1,3:T(8,128)}), f32[1,2,8,32,256]{4,2,0,1,3:T(8,128)S(1)}, u32[]{:S(2)}, u32[]{:S(2)}) async-start(f32[1,2,8,32,256]{4,2,0,1,3:T(8,128)} %copy.25), calls=%async_computation | async-start | bytes 1048576 | tf_op jit(solution)/shard_map/all_to_all | solution.py:37
  117.3 263.4 %all-reduce.4.cloned.1.call-start = ((), (), s32[]{:S(2)}) async-start(), calls=%async_computation.1 | async-start | bytes 524288 | tf_op jit(solution)/shard_map/psum | solution.py:44
Sparse Core Ops, SparseCore 0:
  24.0 80.5 all-reduce.5
  134.1 246.5 all-reduce.3
where the time goes:
time: 479 us
  waiting for transfers between devices  342 us (71%)
  other arithmetic  88.3 us (18%)
  between operations  14.8 us (3%)
  matrix products  12.9 us (3%)
  local copies, waits for them, and re-layouts  11 us (2%)
  starting transfers between devices  10.4 us (2%)
    psum x1, waiting for transfers between devices, local(): gram_sum = lax.psum(product, ('aa', 'ba'))  247 us
    unnamed x3, waiting for transfers between devices  80.2 us
    another operation x4, other arithmetic, local(): lower_factor = jnp.linalg.cholesky(gram_sum)  47.1 us
    another operation x2, other arithmetic, local(): lax.linalg.triangular_solve(lower_factor, identity, left_side=True, lower...  39.4 us
    all_to_all x1, waiting for transfers between devices, local(): lax.all_to_all(block_spec, 'aa', split_axis=3, concat_axis=0, tiled=True)  14.8 us
    all_to_all x1, starting transfers between devices, local(): lax.all_to_all(block_spec, 'aa', split_axis=3, concat_axis=0, tiled=True)  10.1 us
  transfers between devices with their start and end apart: 3, of which 3 were waited for; matrix products, arithmetic and copies ran while one was open for 0% of the time, Pallas kernels for 0%

commit v1 on v0

--- a/solution.py
+++ b/solution.py
@@ -41,7 +41,7 @@
         FREQS, columns, pts_dev
     )
     product = jnp.einsum("fip,fjp->fij", cols, cols, precision=lax.Precision.HIGHEST)
-    gram_sum = lax.psum(product, ("aa", "ba"))
+    gram_sum = lax.psum(lax.psum(product, "ba"), "aa")
     lower_factor = jnp.linalg.cholesky(gram_sum)
     identity = jnp.broadcast_to(jnp.eye(columns, dtype=gram_sum.dtype), lower_factor.shape)
     inverse = lax.linalg.triangular_solve(lower_factor, identity, left_side=True, lower=True)

time: 479 us -> 440 us (0.919)
  waiting for transfers between devices: 342 us -> 287 us
  blocking collectives: 0 us -> 25 us
  starting transfers between devices: 10.4 us -> 0.3 us
    psum x1 -> x2, waiting for transfers between devices: 247 us -> 207 us  [local(): gram_sum = lax.psum(lax.psum(product, 'ba'), 'aa')]
    all_to_all x0 -> x1, blocking collectives: none -> 25 us  [local(): lax.all_to_all(block_spec, 'aa', split_axis=3, concat_axis=0, tiled=True)]
    all_to_all x1 -> x0, waiting for transfers between devices: 14.8 us -> none  [local(): lax.all_to_all(block_spec, 'aa', split_axis=3, concat_axis=0, tiled=True)]
    all_to_all x1 -> x0, starting transfers between devices: 10.1 us -> none  [local(): lax.all_to_all(block_spec, 'aa', split_axis=3, concat_axis=0, tiled=True)]
    unnamed x3 -> x4, waiting for transfers between devices: 80.2 us -> 80.1 us
where the time goes in v1:
time: 440 us; the launch traced here: 439 us
  waiting for transfers between devices  287 us (65%)
  other arithmetic  88.3 us (20%)
  blocking collectives  25 us (6%)
  between operations  14.5 us (3%)
  matrix products  12.9 us (3%)
  local copies, waits for them, and re-layouts  10.2 us (2%)
    psum x2, waiting for transfers between devices, local(): gram_sum = lax.psum(lax.psum(product, 'ba'), 'aa')  207 us
    unnamed x4, waiting for transfers between devices  80.1 us
    another operation x4, other arithmetic, local(): lower_factor = jnp.linalg.cholesky(gram_sum)  47.1 us
    another operation x2, other arithmetic, local(): lax.linalg.triangular_solve(lower_factor, identity, left_side=True, lower...  39.4 us
    all_to_all x1, blocking collectives, local(): lax.all_to_all(block_spec, 'aa', split_axis=3, concat_axis=0, tiled=True)  25 us
    dot_general x1, matrix products, local(): jnp.einsum('savq,sgf->vgfaq', arranged, table, precision=lax.Precision.HI...  9.16 us
    unnamed x6, local copies, waits for them, and re-layouts  9.1 us
  transfers between devices with their start and end apart: 3, of which 3 were waited for; matrix products, arithmetic and copies ran while one was open for 0% of the time, Pallas kernels for 0%

profile of v1, /device:TPU:2, one launch (start us, length us, event | category | flops | bytes accessed | tf_op | source)
XLA Modules:
  0.0 438.5 jit_solution(10516754383478878791)
XLA Ops:
  7.2 0.0 all-reduce.9.cloned.1.call-start
  7.3 0.6 multiply_reduce_fusion
  8.6 5.9 %copy.38 = f32[4,8,256,256]{3,2,1,0:T(8,128)S(1)} copy(f32[4,8,256,256]{3,1,2,0:T(8,128)} %bitcast.42) | data formatting | bytes 16777216
  14.6 0.1 multiply_multiply_fusion.1
  14.7 0.0 copy-start
  14.7 9.2 %fusion.3 = f32[8,2,8,32,256]{4,2,0,3,1:T(8,128)} fusion(f32[32,32,8,256]{3,2,1,0:T(8,128)S(1)} %bitcast.41, f32[32,1,8]{0,2,1:T(8,128)S(1)} %get-tuple-element.13, f32[32,1,8]{0,2,1:T(8,128)S(1)} %get-tuple-element.12), kind=kOutput, calls=%fused_computation.3 | convolution fusion | flops 402653696 | bytes 12584960 | tf_op jit(solution)/shard_map/savq,sgf->vgfaq/dot_general | solution.py:35
  23.9 0.0 all-reduce.9.cloned.1.call-update
  23.9 0.0 all-reduce.5.cloned.1.call-start
  23.9 0.0 copy-done
  24.0 0.6 dynamic-slice
  24.5 80.1 %all-reduce.9.cloned.1.call-done = f32[8,2,8,32,256]{4,2,0,3,1:T(8,128)} async-done(((f32[8,2,8,32,256]{4,2,0,3,1:T(8,128)}), f32[8,2,8,32,256]{4,2,0,3,1:T(8,128)}) %all-reduce.9.cloned.1.call-update) | async-done | bytes 4194320
  104.6 1.7 constant_dynamic-slice_fusion
  106.3 0.1 copy.25
  106.4 25.0 %all_to_all.15 = f32[1,2,8,32,256]{4,2,0,1,3:T(8,128)S(1)} all-to-all(f32[1,2,8,32,256]{4,2,0,1,3:T(8,128)S(1)} %copy.25), channel_id=1, replica_groups=mesh['aa'=32,'ba'=8] {'aa'}, dimensions={3} | all-to-all | bytes 1048576 | tf_op jit(solution)/shard_map/all_to_all | solution.py:37
  131.4 1.6 fusion.7
  133.0 0.0 all-reduce.5.cloned.1.call-update
  133.0 0.2 all-reduce.7.cloned.1.call-start
  133.3 61.3 %all-reduce.5.cloned.1.call-done = f32[8,64,64]{1,2,0:T(8,128)} async-done(((f32[8,64,64]{1,2,0:T(8,128)}), f32[8,64,64]{1,2,0:T(8,128)}) %all-reduce.5.cloned.1.call-update) | async-done | bytes 131088 | tf_op jit(solution)/shard_map/psum | solution.py:44
  194.5 0.0 all-reduce.7.cloned.1.call-update
  194.6 145.8 %all-reduce.7.cloned.1.call-done = f32[8,64,64]{1,2,0:T(8,128)} async-done(((f32[8,64,64]{1,2,0:T(8,128)}), f32[8,64,64]{1,2,0:T(8,128)}) %all-reduce.7.cloned.1.call-update) | async-done | bytes 131088 | tf_op jit(solution)/shard_map/psum | solution.py:44
  340.4 1.1 copy.29
  341.5 1.0 fusion.11
  342.5 46.9 %custom-call.7 = f32[8,64,64]{2,1,0:T(8,128)S(1)} custom-call(f32[8,64,64]{2,1,0:T(8,128)S(1)} %fusion.11), custom_call_target="Cholesky" | custom-call | tf_op jit(solution)/shard_map/jit(cholesky)/cholesky | solution.py:45
  389.5 0.1 compare_reduce_fusion
  389.6 0.1 select_bitcast_fusion
  389.7 39.3 %custom-call.8 = f32[8,1,64,64]{2,3,1,0:T(8,128)S(1)} custom-call(f32[8,1,64,64]{3,2,1,0:T(8,128)S(1)} %get-tuple-element.10), custom_call_target="InvertDiagBlocksLowerTriangular" | custom-call | tf_op jit(solution)/shard_map/triangular_solve | solution.py:47
  429.0 0.6 fusion.9
  429.6 1.5 convolution_multiply_fusion
  431.1 0.8 copy.32
  (7 shorter events, 0.1 us)
Async XLA Ops:
  7.2 97.5 %all-reduce.9.cloned.1.call-start = ((), (), s32[]{:S(2)}) async-start(), calls=%async_computation.3 | async-start | bytes 8388608
  14.7 9.3 %copy-start = (u32[256]{0:T(256)S(1)}, u32[256]{0:T(256)}, u32[]{:S(2)}) copy-start(u32[256]{0:T(256)} %constant.81) | copy-start | bytes 3076
  23.9 170.6 %all-reduce.5.cloned.1.call-start = ((), (), s32[]{:S(2)}) async-start(), calls=%async_computation.1 | async-start | bytes 524288 | tf_op jit(solution)/shard_map/psum | solution.py:44
  133.0 207.4 %all-reduce.7.cloned.1.call-start = ((), (), s32[]{:S(2)}) async-start(), calls=%async_computation.2 | async-start | bytes 524288 | tf_op jit(solution)/shard_map/psum | solution.py:44
Sparse Core Ops, SparseCore 0:
  24.0 80.5 all-reduce.8
  133.1 61.3 all-reduce.4
  198.4 142.0 all-reduce.6

commit v2 on v0

--- a/solution.py
+++ b/solution.py
@@ -34,7 +34,10 @@
     arranged = snapshots.reshape(time_dev, n_aa, n_ba, pts_dev)
     partial = jnp.einsum("savq,sgf->vgfaq", arranged, table, precision=lax.Precision.HIGHEST)
     block_spec = lax.psum_scatter(partial, "ba", scatter_dimension=0, tiled=True)
-    spectra = lax.all_to_all(block_spec, "aa", split_axis=3, concat_axis=0, tiled=True)
+    spectra = jnp.concatenate(
+        lax.all_to_all(jnp.stack(jnp.split(block_spec, lax.axis_size("aa"), axis=3)), "aa", 0, 0),
+        axis=0,
+    )
     blocks = spectra.shape[0]
     columns = 2 * blocks
     cols = jnp.transpose(spectra.reshape(blocks, 2, FREQS, pts_dev), (2, 0, 1, 3)).reshape(

time: 479 us -> 542 us (1.13)
  local copies, waits for them, and re-layouts: 11 us -> 72.1 us
    unnamed x6 -> x36, local copies, waits for them, and re-layouts: 9.1 us -> 69.1 us
where the time goes in v2:
time: 542 us; the launch traced here: 540 us
  waiting for transfers between devices  341 us (63%)
  other arithmetic  88.3 us (16%)
  local copies, waits for them, and re-layouts  72.1 us (13%)
  between operations  14.8 us (3%)
  matrix products  12.9 us (2%)
  starting transfers between devices  10.4 us (2%)
    psum x1, waiting for transfers between devices, local(): gram_sum = lax.psum(product, ('aa', 'ba'))  247 us
    unnamed x3, waiting for transfers between devices  79.5 us
    unnamed x36, local copies, waits for them, and re-layouts  69.1 us
    another operation x4, other arithmetic, local(): lower_factor = jnp.linalg.cholesky(gram_sum)  47.1 us
    another operation x2, other arithmetic, local(): lax.linalg.triangular_solve(lower_factor, identity, left_side=True, lower...  39.4 us
    all_to_all x1, waiting for transfers between devices, local(): lax.all_to_all(jnp.stack(jnp.split(block_spec, lax.axis_size('aa'), axis=...  14.8 us
  transfers between devices with their start and end apart: 3, of which 3 were waited for; matrix products, arithmetic and copies ran while one was open for 0% of the time, Pallas kernels for 0%

profile of v2, /device:TPU:2, one launch (start us, length us, event | category | flops | bytes accessed | tf_op | source)
XLA Modules:
  0.0 539.6 jit_solution(11308106750119786190)
XLA Ops:
  7.2 0.0 all-reduce.6.cloned.1.call-start
  7.3 0.6 multiply_reduce_fusion
  8.6 5.9 %copy.151 = f32[4,8,256,256]{3,2,1,0:T(8,128)S(1)} copy(f32[4,8,256,256]{3,1,2,0:T(8,128)} %bitcast.228) | data formatting | bytes 16777216
  14.6 0.1 multiply_multiply_fusion.1
  14.7 9.2 %fusion.3 = f32[8,2,8,32,256]{4,2,0,3,1:T(8,128)} fusion(f32[32,32,8,256]{3,2,1,0:T(8,128)S(1)} %bitcast.227, f32[32,1,8]{0,2,1:T(8,128)S(1)} %get-tuple-element.11, f32[32,1,8]{0,2,1:T(8,128)S(1)} %get-tuple-element.10), kind=kOutput, calls=%fused_computation.3 | convolution fusion | flops 402653696 | bytes 12584960 | tf_op jit(solution)/shard_map/savq,sgf->vgfaq/dot_general | solution.py:35
  23.9 0.0 copy-start
  23.9 0.0 all-reduce.6.cloned.1.call-update
  23.9 0.6 copy-done
  24.5 0.6 dynamic-slice
  25.1 79.5 %all-reduce.6.cloned.1.call-done = f32[8,2,8,32,256]{4,2,0,3,1:T(8,128)} async-done(((f32[8,2,8,32,256]{4,2,0,3,1:T(8,128)}), f32[8,2,8,32,256]{4,2,0,3,1:T(8,128)}) %all-reduce.6.cloned.1.call-update) | async-done | bytes 4194320
  104.6 2.0 constant_dynamic-update-slice_fusion.31
  106.6 2.0 constant_dynamic-update-slice_fusion.30
  108.6 2.0 constant_dynamic-update-slice_fusion.29
  110.5 2.0 constant_dynamic-update-slice_fusion.28
  112.5 2.0 constant_dynamic-update-slice_fusion.27
  114.5 2.0 constant_dynamic-update-slice_fusion.26
  116.4 2.0 constant_dynamic-update-slice_fusion.25
  118.4 2.0 constant_dynamic-update-slice_fusion.24
  120.4 2.0 constant_dynamic-update-slice_fusion.23
  122.3 2.0 constant_dynamic-update-slice_fusion.22
  124.3 2.0 constant_dynamic-update-slice_fusion.21
  126.3 2.0 constant_dynamic-update-slice_fusion.20
  128.3 2.0 constant_dynamic-update-slice_fusion.19
  130.2 2.0 constant_dynamic-update-slice_fusion.18
  132.2 2.0 constant_dynamic-update-slice_fusion.17
  134.2 2.0 constant_dynamic-update-slice_fusion.16
  136.1 2.0 constant_dynamic-update-slice_fusion.15
  138.1 2.0 constant_dynamic-update-slice_fusion.14
  140.1 2.0 constant_dynamic-update-slice_fusion.13
  142.1 2.0 constant_dynamic-update-slice_fusion.12
  144.0 2.0 constant_dynamic-update-slice_fusion.11
  146.0 2.0 constant_dynamic-update-slice_fusion.10
  148.0 2.0 constant_dynamic-update-slice_fusion.9
  149.9 2.0 constant_dynamic-update-slice_fusion.8
  151.9 2.0 constant_dynamic-update-slice_fusion.7
  153.9 2.0 constant_dynamic-update-slice_fusion.6
  155.8 2.0 constant_dynamic-update-slice_fusion.5
  157.8 2.0 constant_dynamic-update-slice_fusion.4
  159.8 2.0 constant_dynamic-update-slice_fusion.3
  161.8 2.0 constant_dynamic-update-slice_fusion.2
  163.7 2.0 constant_dynamic-update-slice_fusion.1
  165.7 2.0 constant_dynamic-update-slice_fusion
  167.7 10.1 %all-to-all-start = ((f32[32,1,2,8,1,256]{5,3,2,4,1,0:T(8,128)}), f32[32,1,2,8,1,256]{5,3,2,4,1,0:T(8,128)S(1)}, u32[]{:S(2)}, u32[]{:S(2)}) async-start(f32[32,1,2,8,1,256]{5,3,2,4,1,0:T(8,128)} %constant_dynamic-update-slice_fusion), calls=%async_computation | async-start | bytes 1048576 | tf_op jit(solution)/shard_map/all_to_all | solution.py:38
  177.8 0.2 all-reduce.4.cloned.1.call-start
  178.1 14.8 %all-to-all-done = f32[32,1,2,8,1,256]{5,3,2,4,1,0:T(8,128)S(1)} async-done(((f32[32,1,2,8,1,256]{5,3,2,4,1,0:T(8,128)}), f32[32,1,2,8,1,256]{5,3,2,4,1,0:T(8,128)S(1)}, u32[]{:S(2)}, u32[]{:S(2)}) %all-to-all-start) | async-done | bytes 524320 | tf_op jit(solution)/shard_map/all_to_all | solution.py:38
  192.9 1.6 fusion.7
  194.5 0.0 all-reduce.4.cloned.1.call-update
  194.5 246.7 %all-reduce.4.cloned.1.call-done = f32[8,64,64]{1,2,0:T(8,128)} async-done(((f32[8,64,64]{1,2,0:T(8,128)}), f32[8,64,64]{1,2,0:T(8,128)}) %all-reduce.4.cloned.1.call-update) | async-done | bytes 131088 | tf_op jit(solution)/shard_map/psum | solution.py:47
  441.2 1.1 copy.111
  442.3 1.0 fusion.11
  443.3 46.9 %custom-call.7 = f32[8,64,64]{2,1,0:T(8,128)S(1)} custom-call(f32[8,64,64]{2,1,0:T(8,128)S(1)} %fusion.11), custom_call_target="Cholesky" | custom-call | tf_op jit(solution)/shard_map/jit(cholesky)/cholesky | solution.py:48
  490.2 0.1 compare_reduce_fusion
  490.4 0.1 select_bitcast_fusion
  490.5 39.3 %custom-call.8 = f32[8,1,64,64]{2,3,1,0:T(8,128)S(1)} custom-call(f32[8,1,64,64]{3,2,1,0:T(8,128)S(1)} %get-tuple-element.8), custom_call_target="InvertDiagBlocksLowerTriangular" | custom-call | tf_op jit(solution)/shard_map/triangular_solve | solution.py:50
  529.8 0.6 fusion.9
  530.4 1.5 convolution_multiply_fusion
  531.9 0.8 copy.113
  (7 shorter events, 0.1 us)
Async XLA Ops:
  7.2 97.4 %all-reduce.6.cloned.1.call-start = ((), (), s32[]{:S(2)}) async-start(), calls=%async_computation.2 | async-start | bytes 8388608
  23.9 0.7 copy-start
  167.7 25.2 %all-to-all-start = ((f32[32,1,2,8,1,256]{5,3,2,4,1,0:T(8,128)}), f32[32,1,2,8,1,256]{5,3,2,4,1,0:T(8,128)S(1)}, u32[]{:S(2)}, u32[]{:S(2)}) async-start(f32[32,1,2,8,1,256]{5,3,2,4,1,0:T(8,128)} %constant_dynamic-update-slice_fusion), calls=%async_computation | async-start | bytes 1048576 | tf_op jit(solution)/shard_map/all_to_all | solution.py:38
  177.8 263.4 %all-reduce.4.cloned.1.call-start = ((), (), s32[]{:S(2)}) async-start(), calls=%async_computation.1 | async-start | bytes 524288 | tf_op jit(solution)/shard_map/psum | solution.py:47
Sparse Core Ops, SparseCore 0:
  24.0 80.5 all-reduce.5
  194.6 246.5 all-reduce.3
